TPU v7x, 32 devices: a whole 2x2x4 slice. The times are simulated.
32 devices in a mesh: region: 4 (over z), narrow: 8 (over y, x, core).
Axes of the slice: x: 2, y: 2, z: 4, core: 2. Of those that a mesh axis runs over, the one named last changes fastest.
Arguments:
- dust_pos: float32 [3, 6144], P(None, ('region', 'narrow')), may hold values from -1 to 1
- dust_vel: float32 [3, 6144], P(None, ('region', 'narrow')), may hold values from -6 to 6
- dust_tau: float32 [6144], P(('region', 'narrow')), may hold values from 0.02 to 2
- dest: int32 [6144, 1], P(('region', 'narrow')), may hold values from 0 to 3; in each aligned block of 192 rows (0 to 191, 192 to 383, ...) at most 96 rows name the same one
- counts: int32 [32], P(('region', 'narrow')), may hold values from 96 to 192, as said below
- wake_pos: float32 [3, 32768], P(None, ('region', 'narrow')), may hold values from -1 to 1
- wake_gamma: float32 [3, 32768], P(None, ('region', 'narrow')), may hold values from -0.3 to 0.3
- wake_core: float32 [32768], P(('region', 'narrow')), may hold values from 0.05 to 0.3
Outputs:
- moved: float32 [6, 12288], P(None, ('region', 'narrow'))
Inputs may be any that keep to these rules, and one draw needn't show every extreme that they name: `dest`: in each device's 192 rows, no region is named by more than 96 rows, and some device's rows name some region exactly 96 times. `counts`: some device has all its rows live in every draw.
All inputs are finite; a program needn't handle non-finite values.
Results may differ from a plain program's by a relative error of at most 0.0003.
Values sent between devices are 32-bit elements; how exact they have to be, the bound alone decides.
No kernel may reach another device: no remote copies, remote signals or barrier semaphores. Data moves between devices by JAX's collectives and lax.ppermute only.
A program may use at most 64 MiB of HBM per device.

v0:
```python
import math
import jax
import jax.numpy as jnp
from jax import lax
from jax.sharding import PartitionSpec as P

step_size = 0.1
gravity = 1.0


def cross_rows(first, second):
    return jnp.stack(
        [
            first[1] * second[2] - first[2] * second[1],
            first[2] * second[0] - first[0] * second[2],
            first[0] * second[1] - first[1] * second[0],
        ]
    )


def raw_terms(points, wake_block):
    point_count = points.shape[1]
    wake_count = wake_block.shape[1]
    wake_width = math.gcd(wake_count, 2048)
    wake_place = wake_block[0:3]
    vortex_gamma = wake_block[3:6]
    core_square = wake_block[6] * wake_block[6]
    tables = jnp.concatenate([vortex_gamma, cross_rows(vortex_gamma, wake_place)], axis=0)
    place_blocks = wake_place.reshape(3, wake_count // wake_width, wake_width).transpose(1, 0, 2)
    table_blocks = tables.reshape(6, wake_count // wake_width, wake_width).transpose(1, 0, 2)
    core_blocks = core_square.reshape(wake_count // wake_width, wake_width)
    point_blocks = points.reshape(3, point_count // point_count, point_count).transpose(1, 0, 2)

    def one_block(point_group):

        def accumulate(running, parts):
            place_part, table_part, core_part = parts
            first_gap = point_group[0][:, None] - place_part[0][None, :]
            second_gap = point_group[1][:, None] - place_part[1][None, :]
            third_gap = point_group[2][:, None] - place_part[2][None, :]
            distance_sq = (
                first_gap * first_gap
                + second_gap * second_gap
                + third_gap * third_gap
                + core_part[None, :]
            )
            kernel = 1.0 / (distance_sq * jnp.sqrt(distance_sq))
            product = lax.dot_general(
                table_part, kernel, (((1,), (1,)), ((), ())), precision=lax.Precision.HIGHEST
            )
            return (running + product, None)

        total, _ = lax.scan(
            accumulate,
            jnp.zeros((6, point_count), jnp.float32),
            (place_blocks, table_blocks, core_blocks),
        )
        return total

    result = lax.map(one_block, point_blocks)
    return result.transpose(1, 0, 2).reshape(6, point_count)


def advance(arrived, raw_sums):
    points = arrived[0:3]
    velocity = arrived[3:6]
    live_flag = arrived[7]
    wind = (cross_rows(raw_sums[0:3], points) - raw_sums[3:6]) / (4.0 * math.pi)
    safe_tau = jnp.where(live_flag > 0.5, arrived[6], 1.0)
    rate = step_size / safe_tau
    upward = jnp.array([0.0, 0.0, 1.0], jnp.float32)[:, None]
    new_velocity = (velocity + rate[None, :] * wind - step_size * gravity * upward) / (
        1.0 + rate[None, :]
    )
    new_place = points + step_size * new_velocity
    return jnp.concatenate([new_place, new_velocity], axis=0) * live_flag[None, :]


def body(dust_pos, dust_vel, dust_tau, dest, counts, wake_pos, wake_gamma, wake_core):
    per_device = dust_tau.shape[0]
    regions = lax.axis_size("region")
    capacity = 2 * per_device // regions
    slot_count = regions * capacity
    live_rows = (jnp.arange(per_device, dtype=jnp.int32) < counts[0]).astype(jnp.float32)
    target = dest[:, 0]
    onehot = (target[:, None] == jnp.arange(regions, dtype=jnp.int32)[None, :]).astype(jnp.int32)
    slot_rank = jnp.sum((jnp.cumsum(onehot, axis=0) - onehot) * onehot, axis=1)
    column = target * capacity + slot_rank
    placing = (column[:, None] == jnp.arange(slot_count, dtype=jnp.int32)[None, :]).astype(
        jnp.float32
    )
    dust_state = (
        jnp.concatenate(
            [dust_pos, dust_vel, dust_tau[None, :], jnp.ones((1, per_device), jnp.float32)], axis=0
        )
        * live_rows[None, :]
    )
    outgoing = jnp.dot(
        dust_state, placing, precision=lax.Precision.HIGHEST, preferred_element_type=jnp.float32
    )
    arrived = lax.all_to_all(outgoing, "region", split_axis=1, concat_axis=1, tiled=True)
    points = arrived[0:3]
    wake_rows = jnp.concatenate([wake_pos, wake_gamma, wake_core[None, :]], axis=0)
    raw_sums = raw_terms(points, lax.all_gather(wake_rows, "narrow", axis=1, tiled=True))
    return advance(arrived, raw_sums)


def solution(mesh):
    in_specs = (
        P(None, ("region", "narrow")),
        P(None, ("region", "narrow")),
        P(("region", "narrow")),
        P(("region", "narrow"), None),
        P(("region", "narrow")),
        P(None, ("region", "narrow")),
        P(None, ("region", "narrow")),
        P(("region", "narrow")),
    )
    out_specs = P(None, ("region", "narrow"))
    return jax.shard_map(body, mesh=mesh, in_specs=in_specs, out_specs=out_specs, check_vma=False)
```

profile of v0, /device:TPU:0, one launch (start us, length us, event | category | flops | bytes accessed | tf_op | source)
XLA Modules:
  0.0 41.4 jit_solution(17835298949323918834)
XLA Ops:
  0.0 0.0 copy-start.2
  0.0 0.0 copy-start.1
  0.0 0.0 copy-start
  0.0 0.7 %iota_compare_fusion.2 = pred[4,192]{1,0:T(4,128)(4,1)S(1)} fusion(s32[192]{0:T(256)} %bitcast.53), kind=kLoop, calls=%fused_computation.52 | loop fusion | flops 768 | bytes 1536 | tf_op jit(solution)/shard_map/eq | solution.py:86
  0.7 1.2 %reduce-window.6 = s32[4,2,128]{2,1,0:T(2,128)S(1)} reduce-window(s32[4,2,128]{2,1,0:T(2,128)S(1)} %reshape.73, s32[]{:T(128)} %constant.25.clone.1), window={size=1x1x128 pad=0_0x0_0x127_0}, to_apply=%region_0.0 | reduce-window | flops 130048 | bytes 8196 | tf_op jit(solution)/shard_map/reduce-window
  2.0 0.1 slice.176
  2.0 0.1 copy.15
  2.2 0.1 copy.16
  2.3 0.1 add_bitcast_fusion
  2.4 0.7 %fusion.31 = s32[192]{0:T(256)S(1)} fusion(s32[256,4]{0,1:T(4,128)S(1)} %bitcast.52, s32[192]{0:T(256)} %bitcast.54), kind=kLoop, calls=%fused_computation.49 | loop fusion | flops 3648 | bytes 4608 | tf_op jit(solution)/shard_map/reduce_sum | solution.py:87
  3.1 0.7 %multiply_add_fusion.1 = s32[192,1]{0,1:T(1,128)S(1)} fusion(s32[192,1]{0,1:T(1,128)S(1)} %bitcast.57, s32[192,1]{0,1:T(1,128)} %param.14), kind=kLoop, calls=%fused_computation.68 | loop fusion | flops 384 | bytes 2304 | tf_op jit(solution)/shard_map/add | solution.py:88
  4.4 0.1 pad.20.clone
  4.5 1.0 %fusion.18 = f32[8,384]{1,0:T(8,128)S(1)} fusion(s32[192]{0:T(256)S(1)} %bitcast.58, f32[1,192]{1,0:T(1,128)} %bitcast.59, f32[3,192]{1,0:T(4,128)} %param.12, f32[3,192]{1,0:T(4,128)} %param.11, f32[8]{0:T(128)S(1)} %pad.20.clone, f32[192]{0:T(256)S(1)} %compare_convert_fusion), kind=kOutput, calls=%fused_computation.24 | convolution fusion | flops 7157760 | bytes 19232 | tf_op jit(solution)/shard_map/dot_general | solution.py:98
  5.5 0.1 all_to_all.6
  5.6 0.6 %copy.17 = f32[8,4,96]{2,0,1:T(8,128)} copy(f32[8,4,96]{2,1,0:T(4,128)S(1)} %all_to_all.6) | data formatting | bytes 24576 | tf_op jit(solution)/shard_map/all_to_all | solution.py:101
  6.2 6.3 %all-to-all-start = ((f32[8,4,96]{2,0,1:T(8,128)}), f32[8,4,96]{2,0,1:T(8,128)S(1)}, u32[]{:S(2)}, u32[]{:S(2)}) async-start(f32[8,4,96]{2,0,1:T(8,128)} %copy.17), calls=%async_computation | async-start | bytes 32768 | tf_op jit(solution)/shard_map/all_to_all | solution.py:101
  12.5 0.0 copy-done.2
  12.5 0.0 copy-done.1
  12.5 0.0 copy-done
  12.5 9.3 %all_gather.3 = f32[7,8192]{1,0:T(8,128)S(1)} all-gather(f32[7,1024]{1,0:T(8,128)S(1)} %pad_maximum_fusion), channel_id=1, replica_groups=mesh['region'=4,'narrow'=8] {'narrow'}, dimensions={1}, use_global_device_ids=true | all-gather | bytes 258048 | tf_op jit(solution)/shard_map/all_gather | solution.py:104
  21.9 0.3 fusion.20
  22.1 0.1 fusion.36
  22.2 0.1 maximum_bitcast_fusion
  22.3 0.0 all-to-all-done
  22.4 0.1 slice.144
  22.5 0.0 copy-start.3
  22.5 17.6 %while.18 = (s32[]{:T(128)}, f32[6,384]{1,0:T(8,128)S(1)}, f32[4,6,2048]{2,1,0:T(8,128)S(1)}, f32[3,384]{1,0:T(4,128)S(1)}, f32[4,3,2048]{2,1,0:T(4,128)S(1)}, /...) while((s32[]{:T(128)}, f32[6,384]{1,0:T(8,128)S(1)}, ...), condition=%wide.region_4.5_spmd.clone, body=%wide.region_3.4_spmd.clone.sunk | while | flops 65278468 | bytes 200859 | solution.py:53
  22.6 4.3 %fusion.43 = f32[6,384]{1,0:T(8,128)S(1)} fusion(f32[2048]{0:T(1024)S(1)} %bitcast.48, f32[2048]{0:T(1024)S(1)} %bitcast.47, f32[384]{0:T(512)S(1)} %get-tuple-element.159, f32[2048]{0:T(1024)S(1)} %bitcast.46, f32[384]{0:T(512)S(1)} %get-tuple-element.161, f32[2048]{0:T(1024)S(1)} %bitcast.45, f32[384]{0:T(512)S(1)} %get-tuple-element.163, ...), kind=kOutput, calls=%fused_computation.11.clone.1 | convolution fusion | flops 65278464 | bytes 125957 | tf_op jit(solution)/shard_map/while/body/eval_jaxpr/while/body/eval_jaxpr/dot_general | solution.py:48
  27.0 4.3 %fusion.43 = f32[6,384]{1,0:T(8,128)S(1)} fusion(f32[2048]{0:T(1024)S(1)} %bitcast.48, f32[2048]{0:T(1024)S(1)} %bitcast.47, f32[384]{0:T(512)S(1)} %get-tuple-element.159, f32[2048]{0:T(1024)S(1)} %bitcast.46, f32[384]{0:T(512)S(1)} %get-tuple-element.161, f32[2048]{0:T(1024)S(1)} %bitcast.45, f32[384]{0:T(512)S(1)} %get-tuple-element.163, ...), kind=kOutput, calls=%fused_computation.11.clone.1 | convolution fusion | flops 65278464 | bytes 125957 | tf_op jit(solution)/shard_map/while/body/eval_jaxpr/while/body/eval_jaxpr/dot_general | solution.py:48
  31.4 4.3 %fusion.43 = f32[6,384]{1,0:T(8,128)S(1)} fusion(f32[2048]{0:T(1024)S(1)} %bitcast.48, f32[2048]{0:T(1024)S(1)} %bitcast.47, f32[384]{0:T(512)S(1)} %get-tuple-element.159, f32[2048]{0:T(1024)S(1)} %bitcast.46, f32[384]{0:T(512)S(1)} %get-tuple-element.161, f32[2048]{0:T(1024)S(1)} %bitcast.45, f32[384]{0:T(512)S(1)} %get-tuple-element.163, ...), kind=kOutput, calls=%fused_computation.11.clone.1 | convolution fusion | flops 65278464 | bytes 125957 | tf_op jit(solution)/shard_map/while/body/eval_jaxpr/while/body/eval_jaxpr/dot_general | solution.py:48
  35.8 4.3 %fusion.43 = f32[6,384]{1,0:T(8,128)S(1)} fusion(f32[2048]{0:T(1024)S(1)} %bitcast.48, f32[2048]{0:T(1024)S(1)} %bitcast.47, f32[384]{0:T(512)S(1)} %get-tuple-element.159, f32[2048]{0:T(1024)S(1)} %bitcast.46, f32[384]{0:T(512)S(1)} %get-tuple-element.161, f32[2048]{0:T(1024)S(1)} %bitcast.45, f32[384]{0:T(512)S(1)} %get-tuple-element.163, ...), kind=kOutput, calls=%fused_computation.11.clone.1 | convolution fusion | flops 65278464 | bytes 125957 | tf_op jit(solution)/shard_map/while/body/eval_jaxpr/while/body/eval_jaxpr/dot_general | solution.py:48
  40.1 0.1 slice_reduce_fusion.4
  40.1 0.1 slice.158
  40.2 0.1 slice.161
  40.3 0.1 slice.163
  40.4 0.1 slice.167
  40.4 0.1 slice.169
  40.6 0.1 slice.146
  40.7 0.0 copy-done.3
  40.7 0.1 multiply_add_fusion
  40.7 0.6 %maximum_multiply_fusion = f32[6,384]{1,0:T(8,128)} fusion(f32[3,384]{1,0:T(4,128)S(1)} %get-tuple-element.98, f32[3,384]{1,0:T(4,128)S(1)} %get-tuple-element.97, f32[384]{0:T(512)S(1)} %slice.167), kind=kLoop, calls=%fused_computation.33 | loop fusion | flops 4608 | bytes 19968 | tf_op jit(solution)/shard_map/mul | solution.py:76
  (27 shorter events, 0.4 us)
Async XLA Ops:
  0.0 12.5 %copy-start.2 = (f32[1024]{0:T(1024)S(1)}, f32[1024]{0:T(1024)}, u32[]{:S(2)}) copy-start(f32[1024]{0:T(1024)} %param.18) | copy-start | bytes 12292
  0.0 12.5 %copy-start.1 = (f32[3,1024]{1,0:T(4,128)S(1)}, f32[3,1024]{1,0:T(4,128)}, u32[]{:S(2)}) copy-start(f32[3,1024]{1,0:T(4,128)} %param.16) | copy-start | bytes 36868
  0.0 12.5 %copy-start = (f32[3,1024]{1,0:T(4,128)S(1)}, f32[3,1024]{1,0:T(4,128)}, u32[]{:S(2)}) copy-start(f32[3,1024]{1,0:T(4,128)} %param.17) | copy-start | bytes 36868
  6.2 16.2 %all-to-all-start = ((f32[8,4,96]{2,0,1:T(8,128)}), f32[8,4,96]{2,0,1:T(8,128)S(1)}, u32[]{:S(2)}, u32[]{:S(2)}) async-start(f32[8,4,96]{2,0,1:T(8,128)} %copy.17), calls=%async_computation | async-start | bytes 32768 | tf_op jit(solution)/shard_map/all_to_all | solution.py:101
  22.5 18.2 %copy-start.3 = (f32[3]{0:T(128)S(1)}, f32[3]{0:T(128)}, u32[]{:S(2)}) copy-start(f32[3]{0:T(128)} %constant.56) | copy-start | bytes 40
where the time goes:
time: 41.7 us; the launch traced here: 41.4 us
  matrix products  18.2 us (44%)
  blocking collectives  9.32 us (22%)
  starting transfers between devices  6.33 us (15%)
  other arithmetic  4.56 us (11%)
  local copies, waits for them, and re-layouts  2.08 us (5%)
  between operations  0.78 us (2%)
    dot_general x4, matrix products, accumulate(): lax.dot_general(table_part, kernel, (((1,), (1,)), ((), ())), precision=l...  17.2 us
    all_gather x1, blocking collectives, body(): lax.all_gather(wake_rows, 'narrow', axis=1, tiled=True)  9.32 us
    all_to_all x1, starting transfers between devices, body(): lax.all_to_all(outgoing, 'region', split_axis=1, concat_axis=1, tiled=True)  6.33 us
    another operation x3, other arithmetic  1.26 us
    dot_general x1, matrix products, body(): jnp.dot(dust_state, placing, precision=lax.Precision.HIGHEST, preferred_e...  0.99 us
  transfers between devices with their start and end apart: 1, of which 0 were waited for; matrix products, arithmetic and copies ran while one was open for 1% of the time, Pallas kernels for 0%

commit v1 on v0

--- a/solution.py
+++ b/solution.py
@@ -6,6 +6,24 @@
 
 step_size = 0.1
 gravity = 1.0
+
+
+def collect(shard, axis, dim):
+    ways, here, step = (lax.axis_size(axis), lax.axis_index(axis), shard.shape[dim])
+    dims = [n * ways if d == dim else n for d, n in enumerate(shard.shape)]
+    full = lax.dynamic_update_slice_in_dim(
+        jnp.zeros(dims, shard.dtype), shard, here * step, axis=dim
+    )
+    going_up = going_down = shard
+    for far in range(1, ways // 2 + 1):
+        going_up = lax.ppermute(going_up, axis, [(d, (d + 1) % ways) for d in range(ways)])
+        full = lax.dynamic_update_slice_in_dim(full, going_up, (here - far) % ways * step, axis=dim)
+        if 2 * far < ways:
+            going_down = lax.ppermute(going_down, axis, [(d, (d - 1) % ways) for d in range(ways)])
+            full = lax.dynamic_update_slice_in_dim(
+                full, going_down, (here + far) % ways * step, axis=dim
+            )
+    return full
 
 
 def cross_rows(first, second):
@@ -101,7 +119,7 @@
     arrived = lax.all_to_all(outgoing, "region", split_axis=1, concat_axis=1, tiled=True)
     points = arrived[0:3]
     wake_rows = jnp.concatenate([wake_pos, wake_gamma, wake_core[None, :]], axis=0)
-    raw_sums = raw_terms(points, lax.all_gather(wake_rows, "narrow", axis=1, tiled=True))
+    raw_sums = raw_terms(points, collect(wake_rows, "narrow", 1))
     return advance(arrived, raw_sums)
 
 

time: 41.7 us -> 50.7 us (1.22)
  waiting for transfers between devices: 0.01 us -> 10.2 us
  blocking collectives: 9.32 us -> 0 us
  starting transfers between devices: 6.33 us -> 14.3 us
    all_gather x1 -> x0, blocking collectives: 9.32 us -> none  [body(): lax.all_gather(wake_rows, 'narrow', axis=1, tiled=True)]
    ppermute x0 -> x7, starting transfers between devices: none -> 8.02 us  [the longest x3 7.9 us: collect(): lax.ppermute(going_down, axis, [(d, (d - 1) % ways) for d in range(ways)])]
    ppermute x0 -> x7, waiting for transfers between devices: none -> 7.36 us  [the longest x4 7.35 us: collect(): lax.ppermute(going_up, axis, [(d, (d + 1) % ways) for d in range(ways)])]
    all_to_all x1, waiting for transfers between devices: 0.01 us -> 2.83 us  [body(): lax.all_to_all(outgoing, 'region', split_axis=1, concat_axis=1, tiled=True)]
  transfers between devices with their start and end apart: 1 -> 8, of which waited for: 0 -> 4; matrix products, arithmetic and copies ran while one was open for 1% -> 1% of each run, Pallas kernels for 0% -> 0%
where the time goes in v1:
time: 50.7 us; the launch traced here: 50.4 us
  matrix products  18.2 us (36%)
  starting transfers between devices  14.3 us (28%)
  waiting for transfers between devices  10.2 us (20%)
  other arithmetic  4.58 us (9%)
  local copies, waits for them, and re-layouts  2.14 us (4%)
  between operations  0.84 us (2%)
    dot_general x4, matrix products, accumulate(): lax.dot_general(table_part, kernel, (((1,), (1,)), ((), ())), precision=l...  17.2 us
    ppermute x3, starting transfers between devices, collect(): lax.ppermute(going_down, axis, [(d, (d - 1) % ways) for d in range(ways)])  7.9 us
    ppermute x4, waiting for transfers between devices, collect(): lax.ppermute(going_up, axis, [(d, (d + 1) % ways) for d in range(ways)])  7.35 us
    all_to_all x1, starting transfers between devices, body(): lax.all_to_all(outgoing, 'region', split_axis=1, concat_axis=1, tiled=True)  6.32 us
    all_to_all x1, waiting for transfers between devices, body(): lax.all_to_all(outgoing, 'region', split_axis=1, concat_axis=1, tiled=True)  2.83 us
    another operation x3, other arithmetic  1.26 us
  transfers between devices with their start and end apart: 8, of which 4 were waited for; matrix products, arithmetic and copies ran while one was open for 1% of the time, Pallas kernels for 0%

profile of v1, /device:TPU:0, one launch (start us, length us, event | category | flops | bytes accessed | tf_op | source)
XLA Modules:
  0.0 50.4 jit_solution(15386574969976524291)
XLA Ops:
  0.0 0.7 %iota_compare_fusion.2 = pred[4,192]{1,0:T(4,128)(4,1)S(1)} fusion(s32[192]{0:T(256)} %bitcast.53), kind=kLoop, calls=%fused_computation.52 | loop fusion | flops 768 | bytes 1536 | tf_op jit(solution)/shard_map/eq | solution.py:104
  0.7 1.2 %reduce-window.6 = s32[4,2,128]{2,1,0:T(2,128)S(1)} reduce-window(s32[4,2,128]{2,1,0:T(2,128)S(1)} %reshape.73, s32[]{:T(128)} %constant.94.clone.1), window={size=1x1x128 pad=0_0x0_0x127_0}, to_apply=%region_0.0 | reduce-window | flops 130048 | bytes 8196 | tf_op jit(solution)/shard_map/reduce-window
  1.9 0.1 slice.176
  2.0 0.1 copy.15
  2.2 0.1 copy.16
  2.2 0.1 add_bitcast_fusion
  2.3 0.7 %fusion.31 = s32[192]{0:T(256)S(1)} fusion(s32[256,4]{0,1:T(4,128)S(1)} %bitcast.52, s32[192]{0:T(256)} %bitcast.54), kind=kLoop, calls=%fused_computation.49 | loop fusion | flops 3648 | bytes 4608 | tf_op jit(solution)/shard_map/reduce_sum | solution.py:105
  3.1 0.7 %multiply_add_fusion.1 = s32[192,1]{0,1:T(1,128)S(1)} fusion(s32[192,1]{0,1:T(1,128)S(1)} %bitcast.57, s32[192,1]{0,1:T(1,128)} %param.14), kind=kLoop, calls=%fused_computation.76 | loop fusion | flops 384 | bytes 2304 | tf_op jit(solution)/shard_map/add | solution.py:106
  4.4 0.1 pad.20.clone
  4.5 1.0 %fusion.18 = f32[8,384]{1,0:T(8,128)S(1)} fusion(s32[192]{0:T(256)S(1)} %bitcast.58, f32[1,192]{1,0:T(1,128)} %bitcast.59, f32[3,192]{1,0:T(4,128)} %param.12, f32[3,192]{1,0:T(4,128)} %param.11, f32[8]{0:T(128)S(1)} %pad.20.clone, f32[192]{0:T(256)S(1)} %compare_convert_fusion), kind=kOutput, calls=%fused_computation.24 | convolution fusion | flops 7157760 | bytes 19232 | tf_op jit(solution)/shard_map/dot_general | solution.py:116
  5.5 0.1 all_to_all.6
  5.6 0.6 %copy.17 = f32[8,4,96]{2,0,1:T(8,128)} copy(f32[8,4,96]{2,1,0:T(4,128)S(1)} %all_to_all.6) | data formatting | bytes 24576 | tf_op jit(solution)/shard_map/all_to_all | solution.py:119
  6.2 6.3 %all-to-all-start = ((f32[8,4,96]{2,0,1:T(8,128)}), f32[8,4,96]{2,0,1:T(8,128)S(1)}, u32[]{:S(2)}, u32[]{:S(2)}) async-start(f32[8,4,96]{2,0,1:T(8,128)} %copy.17), calls=%async_computation | async-start | bytes 32768 | tf_op jit(solution)/shard_map/all_to_all | solution.py:119
  12.5 0.0 copy-done
  12.6 0.1 collective-permute-start
  12.6 2.6 %collective-permute-start.1 = (f32[7,1024]{1,0:T(8,128)S(1)}, f32[7,1024]{1,0:T(8,128)S(1)}, u32[]{:S(2)}, u32[]{:S(2)}) collective-permute-start(f32[7,1024]{1,0:T(8,128)S(1)} %get-tuple-element.102), channel_id=1, source_target_pairs={{0,7},{1,0},{2,1},{3,2},{4,3},{5,4},{6,5},{7,6},{8,15},{9,8},{10,9... | collective-permute-start | bytes 86024 | tf_op jit(solution)/shard_map/ppermute | solution.py:22
  15.3 2.8 %all-to-all-done = f32[8,4,96]{2,0,1:T(8,128)S(1)} async-done(((f32[8,4,96]{2,0,1:T(8,128)}), f32[8,4,96]{2,0,1:T(8,128)S(1)}, u32[]{:S(2)}, u32[]{:S(2)}) %all-to-all-start) | async-done | bytes 12320 | tf_op jit(solution)/shard_map/all_to_all | solution.py:119
  18.2 0.1 slice.167
  18.2 0.1 slice.169
  18.4 0.1 slice.144
  18.5 0.1 slice.158
  18.5 0.1 slice.161
  18.6 0.1 slice.163
  18.7 0.1 slice.146
  18.8 0.0 collective-permute-done
  18.8 0.1 collective-permute-start.2
  18.9 0.0 collective-permute-done.1
  18.9 2.6 %collective-permute-start.3 = (f32[7,1024]{1,0:T(8,128)S(1)}, f32[7,1024]{1,0:T(8,128)S(1)}, u32[]{:S(2)}, u32[]{:S(2)}) collective-permute-start(f32[7,1024]{1,0:T(8,128)S(1)} %collective-permute-done.1), channel_id=1, source_target_pairs={{0,7},{1,0},{2,1},{3,2},{4,3},{5,4},{6,5},{7,6},{8,15},{9,8},{10,9... | collective-permute-start | bytes 86024 | tf_op jit(solution)/shard_map/ppermute | solution.py:22
  21.5 1.6 %collective-permute-done.2 = f32[7,1024]{1,0:T(8,128)S(1)} collective-permute-done((f32[7,1024]{1,0:T(8,128)S(1)}, f32[7,1024]{1,0:T(8,128)S(1)}, u32[]{:S(2)}, u32[]{:S(2)}) %collective-permute-start.2) | collective-permute-done | bytes 28704 | tf_op jit(solution)/shard_map/ppermute | solution.py:19
  23.1 0.0 collective-permute-start.4
  23.1 0.0 collective-permute-done.3
  23.1 2.6 %collective-permute-start.5 = (f32[7,1024]{1,0:T(8,128)S(1)}, f32[7,1024]{1,0:T(8,128)S(1)}, u32[]{:S(2)}, u32[]{:S(2)}) collective-permute-start(f32[7,1024]{1,0:T(8,128)S(1)} %collective-permute-done.3), channel_id=1, source_target_pairs={{0,7},{1,0},{2,1},{3,2},{4,3},{5,4},{6,5},{7,6},{8,15},{9,8},{10,9... | collective-permute-start | bytes 86024 | tf_op jit(solution)/shard_map/ppermute | solution.py:22
  25.8 1.6 %collective-permute-done.4 = f32[7,1024]{1,0:T(8,128)S(1)} collective-permute-done((f32[7,1024]{1,0:T(8,128)S(1)}, f32[7,1024]{1,0:T(8,128)S(1)}, u32[]{:S(2)}, u32[]{:S(2)}) %collective-permute-start.4) | collective-permute-done | bytes 28704 | tf_op jit(solution)/shard_map/ppermute | solution.py:19
  27.3 0.0 collective-permute-start.6
  27.3 0.0 collective-permute-done.5
  27.4 4.2 %collective-permute-done.6 = f32[7,1024]{1,0:T(8,128)S(1)} collective-permute-done((f32[7,1024]{1,0:T(8,128)S(1)}, f32[7,1024]{1,0:T(8,128)S(1)}, u32[]{:S(2)}, u32[]{:S(2)}) %collective-permute-start.6) | collective-permute-done | bytes 28704 | tf_op jit(solution)/shard_map/ppermute | solution.py:19
  31.6 0.1 fusion.36
  31.6 0.3 fusion.20
  31.9 0.1 maximum_bitcast_fusion
  32.1 0.0 copy-start.3
  32.1 17.6 %while.18 = (s32[]{:T(128)}, f32[6,384]{1,0:T(8,128)S(1)}, f32[4,6,2048]{2,1,0:T(8,128)S(1)}, f32[3,384]{1,0:T(4,128)S(1)}, f32[4,3,2048]{2,1,0:T(4,128)S(1)}, /...) while((s32[]{:T(128)}, f32[6,384]{1,0:T(8,128)S(1)}, ...), condition=%wide.region_4.5_spmd.clone, body=%wide.region_3.4_spmd.clone.sunk | while | flops 65278468 | bytes 200859 | solution.py:71
  32.2 4.3 %fusion.43 = f32[6,384]{1,0:T(8,128)S(1)} fusion(f32[2048]{0:T(1024)S(1)} %bitcast.48, f32[2048]{0:T(1024)S(1)} %bitcast.47, f32[384]{0:T(512)S(1)} %get-tuple-element.161, f32[2048]{0:T(1024)S(1)} %bitcast.46, f32[384]{0:T(512)S(1)} %get-tuple-element.163, f32[2048]{0:T(1024)S(1)} %bitcast.45, f32[384]{0:T(512)S(1)} %get-tuple-element.165, ...), kind=kOutput, calls=%fused_computation.11.clone.1 | convolution fusion | flops 65278464 | bytes 125957 | tf_op jit(solution)/shard_map/while/body/eval_jaxpr/while/body/eval_jaxpr/dot_general | solution.py:66
  36.6 4.3 %fusion.43 = f32[6,384]{1,0:T(8,128)S(1)} fusion(f32[2048]{0:T(1024)S(1)} %bitcast.48, f32[2048]{0:T(1024)S(1)} %bitcast.47, f32[384]{0:T(512)S(1)} %get-tuple-element.161, f32[2048]{0:T(1024)S(1)} %bitcast.46, f32[384]{0:T(512)S(1)} %get-tuple-element.163, f32[2048]{0:T(1024)S(1)} %bitcast.45, f32[384]{0:T(512)S(1)} %get-tuple-element.165, ...), kind=kOutput, calls=%fused_computation.11.clone.1 | convolution fusion | flops 65278464 | bytes 125957 | tf_op jit(solution)/shard_map/while/body/eval_jaxpr/while/body/eval_jaxpr/dot_general | solution.py:66
  41.0 4.3 %fusion.43 = f32[6,384]{1,0:T(8,128)S(1)} fusion(f32[2048]{0:T(1024)S(1)} %bitcast.48, f32[2048]{0:T(1024)S(1)} %bitcast.47, f32[384]{0:T(512)S(1)} %get-tuple-element.161, f32[2048]{0:T(1024)S(1)} %bitcast.46, f32[384]{0:T(512)S(1)} %get-tuple-element.163, f32[2048]{0:T(1024)S(1)} %bitcast.45, f32[384]{0:T(512)S(1)} %get-tuple-element.165, ...), kind=kOutput, calls=%fused_computation.11.clone.1 | convolution fusion | flops 65278464 | bytes 125957 | tf_op jit(solution)/shard_map/while/body/eval_jaxpr/while/body/eval_jaxpr/dot_general | solution.py:66
  45.4 4.3 %fusion.43 = f32[6,384]{1,0:T(8,128)S(1)} fusion(f32[2048]{0:T(1024)S(1)} %bitcast.48, f32[2048]{0:T(1024)S(1)} %bitcast.47, f32[384]{0:T(512)S(1)} %get-tuple-element.161, f32[2048]{0:T(1024)S(1)} %bitcast.46, f32[384]{0:T(512)S(1)} %get-tuple-element.163, f32[2048]{0:T(1024)S(1)} %bitcast.45, f32[384]{0:T(512)S(1)} %get-tuple-element.165, ...), kind=kOutput, calls=%fused_computation.11.clone.1 | convolution fusion | flops 65278464 | bytes 125957 | tf_op jit(solution)/shard_map/while/body/eval_jaxpr/while/body/eval_jaxpr/dot_general | solution.py:66
  49.7 0.0 copy-done.3
  49.7 0.1 multiply_add_fusion
  49.8 0.6 %maximum_multiply_fusion = f32[6,384]{1,0:T(8,128)} fusion(f32[3,384]{1,0:T(4,128)S(1)} %get-tuple-element.98, f32[3,384]{1,0:T(4,128)S(1)} %get-tuple-element.97, f32[384]{0:T(512)S(1)} %slice.167), kind=kLoop, calls=%fused_computation.33 | loop fusion | flops 4608 | bytes 19968 | tf_op jit(solution)/shard_map/mul | solution.py:94
  (41 shorter events, 0.6 us)
Async XLA Ops:
  2.3 10.2 %copy-start = (f32[3,1024]{1,0:T(4,128)S(1)}, f32[3,1024]{1,0:T(4,128)}, u32[]{:S(2)}) copy-start(f32[3,1024]{1,0:T(4,128)} %param.17) | copy-start | bytes 36868
  2.3 10.2 %copy-start.1 = (f32[3,1024]{1,0:T(4,128)S(1)}, f32[3,1024]{1,0:T(4,128)}, u32[]{:S(2)}) copy-start(f32[3,1024]{1,0:T(4,128)} %param.16) | copy-start | bytes 36868
  2.3 10.2 %copy-start.2 = (f32[1024]{0:T(1024)S(1)}, f32[1024]{0:T(1024)}, u32[]{:S(2)}) copy-start(f32[1024]{0:T(1024)} %param.18) | copy-start | bytes 12292
  6.2 11.9 %all-to-all-start = ((f32[8,4,96]{2,0,1:T(8,128)}), f32[8,4,96]{2,0,1:T(8,128)S(1)}, u32[]{:S(2)}, u32[]{:S(2)}) async-start(f32[8,4,96]{2,0,1:T(8,128)} %copy.17), calls=%async_computation | async-start | bytes 32768 | tf_op jit(solution)/shard_map/all_to_all | solution.py:119
  12.6 6.2 %collective-permute-start = (f32[7,1024]{1,0:T(8,128)S(1)}, f32[7,1024]{1,0:T(8,128)S(1)}, u32[]{:S(2)}, u32[]{:S(2)}) collective-permute-start(f32[7,1024]{1,0:T(8,128)S(1)} %get-tuple-element.102), channel_id=1, source_target_pairs={{0,1},{1,2},{2,3},{3,4},{4,5},{5,6},{6,7},{7,0},{8,9},{9,10},{10,1... | collective-permute-start | bytes 86024 | tf_op jit(solution)/shard_map/ppermute | solution.py:19
  12.6 6.2 %collective-permute-start.1 = (f32[7,1024]{1,0:T(8,128)S(1)}, f32[7,1024]{1,0:T(8,128)S(1)}, u32[]{:S(2)}, u32[]{:S(2)}) collective-permute-start(f32[7,1024]{1,0:T(8,128)S(1)} %get-tuple-element.102), channel_id=1, source_target_pairs={{0,7},{1,0},{2,1},{3,2},{4,3},{5,4},{6,5},{7,6},{8,15},{9,8},{10,9... | collective-permute-start | bytes 86024 | tf_op jit(solution)/shard_map/ppermute | solution.py:22
  18.8 4.3 %collective-permute-start.2 = (f32[7,1024]{1,0:T(8,128)S(1)}, f32[7,1024]{1,0:T(8,128)S(1)}, u32[]{:S(2)}, u32[]{:S(2)}) collective-permute-start(f32[7,1024]{1,0:T(8,128)S(1)} %collective-permute-done), channel_id=1, source_target_pairs={{0,1},{1,2},{2,3},{3,4},{4,5},{5,6},{6,7},{7,0},{8,9},{9,10},{10,1... | collective-permute-start | bytes 86024 | tf_op jit(solution)/shard_map/ppermute | solution.py:19
  18.9 4.2 %collective-permute-start.3 = (f32[7,1024]{1,0:T(8,128)S(1)}, f32[7,1024]{1,0:T(8,128)S(1)}, u32[]{:S(2)}, u32[]{:S(2)}) collective-permute-start(f32[7,1024]{1,0:T(8,128)S(1)} %collective-permute-done.1), channel_id=1, source_target_pairs={{0,7},{1,0},{2,1},{3,2},{4,3},{5,4},{6,5},{7,6},{8,15},{9,8},{10,9... | collective-permute-start | bytes 86024 | tf_op jit(solution)/shard_map/ppermute | solution.py:22
  23.1 4.2 %collective-permute-start.4 = (f32[7,1024]{1,0:T(8,128)S(1)}, f32[7,1024]{1,0:T(8,128)S(1)}, u32[]{:S(2)}, u32[]{:S(2)}) collective-permute-start(f32[7,1024]{1,0:T(8,128)S(1)} %collective-permute-done.2), channel_id=1, source_target_pairs={{0,1},{1,2},{2,3},{3,4},{4,5},{5,6},{6,7},{7,0},{8,9},{9,10},{10,1... | collective-permute-start | bytes 86024 | tf_op jit(solution)/shard_map/ppermute | solution.py:19
  23.1 4.2 %collective-permute-start.5 = (f32[7,1024]{1,0:T(8,128)S(1)}, f32[7,1024]{1,0:T(8,128)S(1)}, u32[]{:S(2)}, u32[]{:S(2)}) collective-permute-start(f32[7,1024]{1,0:T(8,128)S(1)} %collective-permute-done.3), channel_id=1, source_target_pairs={{0,7},{1,0},{2,1},{3,2},{4,3},{5,4},{6,5},{7,6},{8,15},{9,8},{10,9... | collective-permute-start | bytes 86024 | tf_op jit(solution)/shard_map/ppermute | solution.py:22
  27.3 4.2 %collective-permute-start.6 = (f32[7,1024]{1,0:T(8,128)S(1)}, f32[7,1024]{1,0:T(8,128)S(1)}, u32[]{:S(2)}, u32[]{:S(2)}) collective-permute-start(f32[7,1024]{1,0:T(8,128)S(1)} %collective-permute-done.4), channel_id=1, source_target_pairs={{0,1},{1,2},{2,3},{3,4},{4,5},{5,6},{6,7},{7,0},{8,9},{9,10},{10,1... | collective-permute-start | bytes 86024 | tf_op jit(solution)/shard_map/ppermute | solution.py:19
  32.1 17.6 %copy-start.3 = (f32[3]{0:T(128)S(1)}, f32[3]{0:T(128)}, u32[]{:S(2)}) copy-start(f32[3]{0:T(128)} %constant.116) | copy-start | bytes 40
